TPU v7x, 128 devices: a whole 4x4x4 slice. The times are simulated.
128 devices in a mesh: serve: 8 (over x, core), store: 16 (over z, y).
Axes of the slice: x: 4, y: 4, z: 4, core: 2. Of those that a mesh axis runs over, the one named last changes fastest.
Arguments:
- normalized_hidden_states: bfloat16 [65536, 2048], P(('serve', 'store')), may hold values from -20 to 20
- query_weight_matrix: bfloat16 [2048, 2048], replicated, may hold values from -0.125 to 0.125
- key_weight_matrix: bfloat16 [2048, 512], replicated, may hold values from -0.125 to 0.125
- value_weight_matrix: bfloat16 [2048, 512], replicated, may hold values from -0.125 to 0.125
- adapter_down_weight: bfloat16 [512, 32, 2048], P('store', None, 'serve'), may hold values from -0.125 to 0.125
- adapter_up_query_weight: bfloat16 [512, 16, 2048], P('store', None, 'serve'), may hold values from -1.5 to 1.5
- adapter_up_value_weight: bfloat16 [512, 16, 512], P('store', None, 'serve'), may hold values from -1.5 to 1.5
- adapter_panel_slot: int32 [512], replicated, may hold values from 0 to 511, as said below
- adapter_per_request: int32 [128, 16], P(('serve', 'store')), may hold values from 0 to 511, as said below
- request_token_length: int32 [128, 16], P(('serve', 'store')), may hold values from 1 to 64, 512 in all within a row
Outputs:
- attended: bfloat16 [65536, 2048], P(('serve', 'store'))
Inputs may be any that keep to these rules, and one draw needn't show every extreme that they name: Each number appears once; adapter a's panels are entry adapter_panel_slot[a] of the three panel arrays, whose owner is index adapter_panel_slot[a] // 32 of store. `adapter_per_request`: the 16 requests of one device use adapters of 16 different owners. `request_token_length`: each row sums to 512; the longest request of each device has exactly 64 tokens.
All inputs are finite; a program needn't handle non-finite values.
Results may differ from a plain program's by a relative error of at most 0.012.
Values may be sent and summed in bfloat16 or wider, within the bound.
No kernel may reach another device: no remote copies, remote signals or barrier semaphores. Data moves between devices by JAX's collectives and lax.ppermute only.
A program may use at most 128 MiB of HBM per device.

v0:
```python
import jax
import jax.numpy as jnp
from jax import lax
from jax.sharding import PartitionSpec as P

HEADS = 32
KV_HEADS = 8
HEAD_DIM = 64
ADAPTER_RANK = 16
ADP_DEV = 32
LEN_MAX = 64


def rotary(heads_in, positions):
    half_dim = HEAD_DIM // 2
    frequency = 500000.0 ** (-(jnp.arange(half_dim).astype(jnp.float32) * 2.0 / HEAD_DIM))
    angles = positions.astype(jnp.float32)[:, None] * frequency[None, :]
    cosine_table = jnp.cos(angles)[:, None, :]
    sine_table = jnp.sin(angles)[:, None, :]
    first_half = heads_in[..., :half_dim]
    second_half = heads_in[..., half_dim:]
    return jnp.concatenate(
        [
            first_half * cosine_table - second_half * sine_table,
            second_half * cosine_table + first_half * sine_table,
        ],
        axis=-1,
    )


def table_lookup(table, wanted):
    entries = jnp.arange(table.shape[0], dtype=jnp.int32)
    return jnp.sum(jnp.where(wanted[..., None] == entries, table, 0), axis=-1)


def reduced_rank_products(block_list, down_panels, up_query, up_value):
    low = jnp.einsum(
        "jkd,jrd->jkr", block_list, down_panels, preferred_element_type=jnp.float32
    ).astype(jnp.bfloat16)
    query_update = jnp.einsum(
        "jkr,jrd->jkd", low[..., :ADAPTER_RANK], up_query, preferred_element_type=jnp.float32
    ).astype(jnp.bfloat16)
    value_update = jnp.einsum(
        "jkr,jrd->jkd", low[..., ADAPTER_RANK:], up_value, preferred_element_type=jnp.float32
    ).astype(jnp.bfloat16)
    return (query_update, value_update)


def local_choice(panel_set, lists, adapter_panel_slot, my_store):
    source_slots = table_lookup(adapter_panel_slot, lists)
    mine_mask = source_slots // ADP_DEV == my_store
    local_source = jnp.sum(jnp.where(mine_mask, source_slots % ADP_DEV, 0), axis=1)
    return tuple((jnp.take(panel, local_source, axis=0) for panel in panel_set))


def attention(query_rot, key_rot, value_rows, request_ids):
    tok_rows = query_rot.shape[0]
    per_group = HEADS // KV_HEADS
    block_rows = min(128, tok_rows)
    reach = LEN_MAX
    key_pad = jnp.concatenate(
        [jnp.zeros((reach,) + key_rot.shape[1:], key_rot.dtype), key_rot], axis=0
    )
    value_pad = jnp.concatenate(
        [jnp.zeros((reach,) + value_rows.shape[1:], value_rows.dtype), value_rows], axis=0
    )
    ids_pad = jnp.concatenate([jnp.full((reach,), -1, jnp.int32), request_ids], axis=0)
    token_order = jnp.arange(tok_rows, dtype=jnp.int32)
    order_pad = jnp.concatenate([jnp.full((reach,), -1, jnp.int32), token_order], axis=0)
    outputs = []
    for block_index in range(tok_rows // block_rows):
        first = block_index * block_rows
        query_block = query_rot[first : first + block_rows]
        query_ids = request_ids[first : first + block_rows]
        query_order = token_order[first : first + block_rows]
        key_block = key_pad[first : first + reach + block_rows]
        value_block = value_pad[first : first + reach + block_rows]
        key_ids = ids_pad[first : first + reach + block_rows]
        key_order = order_pad[first : first + reach + block_rows]
        allowed = (query_ids[:, None] == key_ids[None, :]) & (
            key_order[None, :] <= query_order[:, None]
        )
        pieces = []
        for group_index in range(KV_HEADS):
            query_part = query_block[:, group_index * per_group : (group_index + 1) * per_group, :]
            key_part = key_block[:, group_index, :]
            value_part = value_block[:, group_index, :]
            scores = jnp.einsum(
                "qhd,kd->hqk", query_part, key_part, preferred_element_type=jnp.float32
            ) * HEAD_DIM ** (-0.5)
            scores = jnp.where(allowed[None], scores, -jnp.inf)
            row_max = jnp.max(scores, axis=-1, keepdims=True)
            raised = jnp.exp(scores - row_max)
            row_total = jnp.sum(raised, axis=-1)
            weights = raised.astype(jnp.bfloat16)
            mixed_heads = (
                jnp.einsum("hqk,kd->qhd", weights, value_part, preferred_element_type=jnp.float32)
                / jnp.transpose(row_total)[:, :, None]
            )
            pieces.append(mixed_heads)
        outputs.append(
            jnp.concatenate(pieces, axis=1)
            .reshape(block_rows, HEADS * HEAD_DIM)
            .astype(jnp.bfloat16)
        )
    return jnp.concatenate(outputs, axis=0)


def local(
    normalized_hidden_states,
    query_weight_matrix,
    key_weight_matrix,
    value_weight_matrix,
    adapter_down_weight,
    adapter_up_query_weight,
    adapter_up_value_weight,
    adapter_panel_slot,
    adapter_per_request,
    request_token_length,
):
    store_count = lax.axis_size("store")
    my_store = lax.axis_index("store")
    tok_rows = normalized_hidden_states.shape[0]
    request_count = request_token_length.shape[1]
    group_lists = lax.all_gather(adapter_per_request, "store", axis=0, tiled=True)
    lengths = request_token_length[0]
    adapters = adapter_per_request[0]
    request_ends = jnp.cumsum(lengths)
    starts = request_ends - lengths
    token_order = jnp.arange(tok_rows, dtype=jnp.int32)
    request_ids = jnp.sum((token_order[:, None] >= request_ends[None, :]).astype(jnp.int32), axis=1)
    member = request_ids[:, None] == jnp.arange(request_count, dtype=jnp.int32)[None, :]
    positions = token_order - jnp.sum(jnp.where(member, starts[None, :], 0), axis=1)
    slot_index_list = table_lookup(adapter_panel_slot, adapters)
    owners = slot_index_list // ADP_DEV
    owner_pick = owners[None, :] == jnp.arange(store_count, dtype=jnp.int32)[:, None]
    start_for = jnp.sum(jnp.where(owner_pick, starts[None, :], 0), axis=1)
    length_for = jnp.sum(jnp.where(owner_pick, lengths[None, :], 0), axis=1)
    offsets = jnp.arange(LEN_MAX, dtype=jnp.int32)
    valid_rows = offsets[None, :] < length_for[:, None]
    row_index = jnp.where(valid_rows, start_for[:, None] + offsets[None, :], 0)
    block_list = jnp.where(
        valid_rows[..., None], normalized_hidden_states[row_index], jnp.zeros((), jnp.bfloat16)
    )
    owner_token = jnp.sum(jnp.where(member, owners[None, :], 0), axis=1)
    back_index = owner_token * LEN_MAX + positions
    panels = (
        lax.all_gather(adapter_down_weight, "serve", axis=2, tiled=True),
        lax.all_gather(adapter_up_query_weight, "serve", axis=2, tiled=True),
        lax.all_gather(adapter_up_value_weight, "serve", axis=2, tiled=True),
    )
    down_chosen, upq_chosen, upv_chosen = local_choice(
        panels, group_lists, adapter_panel_slot, my_store
    )
    arrived = lax.all_to_all(block_list, "store", split_axis=0, concat_axis=0, tiled=True)
    query_update, value_update = reduced_rank_products(arrived, down_chosen, upq_chosen, upv_chosen)
    query_update, value_update = (
        lax.all_to_all(query_update, "store", split_axis=0, concat_axis=0, tiled=True),
        lax.all_to_all(value_update, "store", split_axis=0, concat_axis=0, tiled=True),
    )
    delta_query = query_update.reshape(-1, query_update.shape[2])[back_index]
    delta_value = value_update.reshape(-1, value_update.shape[2])[back_index]
    base_query = jnp.dot(
        normalized_hidden_states, query_weight_matrix, preferred_element_type=jnp.float32
    ) + delta_query.astype(jnp.float32)
    query_rot = rotary(base_query.reshape(tok_rows, HEADS, HEAD_DIM), positions).astype(
        jnp.bfloat16
    )
    base_key = jnp.dot(
        normalized_hidden_states, key_weight_matrix, preferred_element_type=jnp.float32
    )
    key_rot = rotary(base_key.reshape(tok_rows, KV_HEADS, HEAD_DIM), positions).astype(jnp.bfloat16)
    value_rows = (
        jnp.dot(normalized_hidden_states, value_weight_matrix, preferred_element_type=jnp.float32)
        + delta_value.astype(jnp.float32)
    ).astype(jnp.bfloat16)
    value_rows = value_rows.reshape(tok_rows, KV_HEADS, HEAD_DIM)
    return attention(query_rot, key_rot, value_rows, request_ids)


def solution(mesh):
    return jax.shard_map(
        local,
        mesh=mesh,
        in_specs=(
            P(("serve", "store"), None),
            P(),
            P(),
            P(),
            P("store", None, "serve"),
            P("store", None, "serve"),
            P("store", None, "serve"),
            P(),
            P(("serve", "store"), None),
            P(("serve", "store"), None),
        ),
        out_specs=P(("serve", "store"), None),
        check_vma=False,
    )
```

profile of v0, /device:TPU:6, one launch (start us, length us, event | category | flops | bytes accessed | tf_op | source)
XLA Modules:
  0.0 278.1 jit_solution(15129915523642141510)
XLA Ops:
  10.6 6.1 %gather_fusion = bf16[1024,2048]{1,0:T(8,128)(2,1)} fusion(bf16[512,2048]{1,0:T(8,128)(2,1)S(1)} %copy-done, s32[1024]{0:T(1024)S(1)} %broadcast_clamp_fusion), kind=kCustom, calls=%fused_computation | custom fusion | bytes 8392704 | tf_op jit(solution)/shard_map/gather | solution.py:143
  16.8 4.5 %broadcast_select_fusion = bf16[16,64,2048]{2,1,0:T(8,128)(2,1)} fusion(bf16[16,64,2048]{2,1,0:T(8,128)(2,1)} %bitcast.784, pred[16,64]{1,0:T(8,128)(4,1)S(1)} %iota_compare_fusion.6), kind=kLoop, calls=%fused_computation.69 | loop fusion | flops 2097152 | bytes 8389632 | tf_op jit(solution)/shard_map/jit(_where)/select_n | solution.py:142
  21.3 8.3 %all-to-all-start = ((bf16[16,64,2048]{2,1,0:T(8,128)(2,1)}), bf16[16,64,2048]{2,1,0:T(8,128)(2,1)}, u32[]{:S(2)}, u32[]{:S(2)}) async-start(bf16[16,64,2048]{2,1,0:T(8,128)(2,1)} %broadcast_select_fusion), calls=%async_computation | async-start | bytes 8388608 | tf_op jit(solution)/shard_map/all_to_all | solution.py:155
  30.6 21.4 %all_gather.14 = bf16[32,16,512]{0,1,2:T(8,128)(2,1)} all-gather(bf16[32,16,64]{0,1,2:T(8,128)(2,1)S(1)} %copy.78), channel_id=1, replica_groups=mesh['serve'=8,'store'=16] {'serve'}, dimensions={2}, use_global_device_ids=true | all-gather | bytes 589824 | tf_op jit(solution)/shard_map/all_gather | solution.py:150
  52.1 3.1 %copy.79 = bf16[32,16,512]{2,1,0:T(8,128)(2,1)S(1)} copy(bf16[32,16,512]{0,1,2:T(8,128)(2,1)} %all_gather.14) | data formatting | bytes 1048576 | tf_op jit(solution)/shard_map/all_gather | solution.py:150
  55.2 48.8 %all-gather = s32[16,1,16]{2,1,0:T(1,128)S(1)} all-gather(s32[1,1,16]{2,1,0:T(1,128)S(1)} %bitcast.854), channel_id=1, replica_groups=mesh['serve'=8,'store'=16] {'store'}, dimensions={0}, use_global_device_ids=true | all-gather | bytes 1088 | tf_op jit(solution)/shard_map/all_gather | solution.py:125
  105.2 4.2 %gather_fusion.1 = bf16[16,32,2048]{2,1,0:T(8,128)(2,1)} fusion(bf16[32,32,2048]{2,1,0:T(8,128)(2,1)} %all-gather.4.cloned.1.call-done, s32[1024]{0:T(1024)S(1)} %pad_clamp_fusion.1), kind=kCustom, calls=%fused_computation.1 | custom fusion | bytes 4194368 | tf_op jit(solution)/shard_map/jit(_take)/gather | solution.py:53
  109.4 4.1 %fusion.68 = bf16[16,64,32]{1,2,0:T(8,128)(2,1)S(1)} fusion(bf16[16,64,2048]{2,1,0:T(8,128)(2,1)} %all-to-all-done, bf16[16,32,2048]{2,1,0:T(8,128)(2,1)} %gather_fusion.1, pred[16]{0:T(512)(128)(4,1)S(1)} %compare_and_fusion.4), kind=kOutput, calls=%fused_computation.225 | convolution fusion | flops 135299072 | bytes 6357008 | tf_op jit(solution)/shard_map/jkd,jrd->jkr/dot_general | solution.py:37
  115.0 4.6 %all-to-all-start.1 = ((bf16[16,64,512]{2,1,0:T(8,128)(2,1)}), bf16[16,64,512]{2,1,0:T(8,128)(2,1)}, u32[]{:S(2)}, u32[]{:S(2)}) async-start(bf16[16,64,512]{2,1,0:T(8,128)(2,1)} %convolution_convert_fusion.1), calls=%async_computation.1 | async-start | bytes 2097152 | tf_op jit(solution)/shard_map/all_to_all | solution.py:159
  119.7 3.2 %gather_fusion.4 = bf16[16,16,2048]{2,1,0:T(8,128)(2,1)} fusion(bf16[32,16,2048]{2,1,0:T(8,128)(2,1)} %all-gather.6.cloned.1.call-done, s32[1024]{0:T(1024)S(1)} %pad_clamp_fusion.1), kind=kCustom, calls=%fused_computation.4 | custom fusion | bytes 2097216 | tf_op jit(solution)/shard_map/jit(_take)/gather | solution.py:53
  122.8 4.5 %convolution_convert_fusion = bf16[16,64,2048]{2,1,0:T(8,128)(2,1)} fusion(bf16[16,16,2048]{2,1,0:T(8,128)(2,1)} %gather_fusion.4, pred[16]{0:T(512)(128)(4,1)S(1)} %compare_and_fusion.4, bf16[16,64,32]{1,2,0:T(8,128)(2,1)S(1)} %fusion.68), kind=kOutput, calls=%fused_computation.70 | convolution fusion | flops 69730304 | bytes 5308928 | tf_op jit(solution)/shard_map/jkr,jrd->jkd/dot_general | solution.py:40
  127.3 6.5 %all-to-all-done.1 = bf16[16,64,512]{2,1,0:T(8,128)(2,1)} async-done(((bf16[16,64,512]{2,1,0:T(8,128)(2,1)}), bf16[16,64,512]{2,1,0:T(8,128)(2,1)}, u32[]{:S(2)}, u32[]{:S(2)}) %all-to-all-start.1) | async-done | bytes 1048608 | tf_op jit(solution)/shard_map/all_to_all | solution.py:159
  133.8 4.7 %all-to-all-start.2 = ((bf16[16,64,2048]{2,1,0:T(8,128)(2,1)}), bf16[16,64,2048]{2,1,0:T(8,128)(2,1)}, u32[]{:S(2)}, u32[]{:S(2)}) async-start(bf16[16,64,2048]{2,1,0:T(8,128)(2,1)} %convolution_convert_fusion), calls=%async_computation.2 | async-start | bytes 8388608 | tf_op jit(solution)/shard_map/all_to_all | solution.py:158
  139.3 2.9 %fusion.563 = f32[512,512]{0,1:T(8,128)S(1)} fusion(bf16[512,2048]{1,0:T(8,128)(2,1)S(1)} %copy-done, bf16[2048,512]{1,0:T(8,128)(2,1)} %param.12), kind=kOutput, calls=%fused_computation.765 | convolution fusion | flops 1073741824 | bytes 5242880 | tf_op jit(solution)/shard_map/dot_general | solution.py:169
  143.7 3.3 %gather_fusion.3 = bf16[512,512]{1,0:T(8,128)(2,1)S(1)} fusion(bf16[1024,512]{1,0:T(8,128)(2,1)} %bitcast.9, s32[1024]{0:T(1024)S(1)} %pad_clamp_fusion), kind=kCustom, calls=%fused_computation.3 | custom fusion | bytes 1050624 | tf_op jit(solution)/shard_map/gather | solution.py:162
  147.1 3.6 %fusion.3 = bf16[512,512]{1,0:T(8,128)(2,1)} fusion(bf16[512,2048]{1,0:T(8,128)(2,1)S(1)} %copy-done, bf16[2048,512]{1,0:T(8,128)(2,1)} %param.13, bf16[512,512]{1,0:T(8,128)(2,1)S(1)} %gather_fusion.3), kind=kOutput, calls=%fused_computation.128 | convolution fusion | flops 1074528256 | bytes 5242880 | tf_op jit(solution)/shard_map/dot_general | solution.py:174
  159.2 30.4 %all-to-all-done.2 = bf16[16,64,2048]{2,1,0:T(8,128)(2,1)} async-done(((bf16[16,64,2048]{2,1,0:T(8,128)(2,1)}), bf16[16,64,2048]{2,1,0:T(8,128)(2,1)}, u32[]{:S(2)}, u32[]{:S(2)}) %all-to-all-start.2) | async-done | bytes 4194336 | tf_op jit(solution)/shard_map/all_to_all | solution.py:158
  189.6 8.0 %gather_fusion.5 = bf16[512,2048]{1,0:T(8,128)(2,1)} fusion(bf16[1024,2048]{1,0:T(8,128)(2,1)} %bitcast.19, s32[1024]{0:T(1024)S(1)} %pad_clamp_fusion), kind=kCustom, calls=%fused_computation.5 | custom fusion | bytes 4196352 | tf_op jit(solution)/shard_map/gather | solution.py:161
  197.5 9.7 %convert_add_fusion = f32[512,2048]{1,0:T(8,128)} fusion(bf16[512,2048]{1,0:T(8,128)(2,1)} %gather_fusion.5, bf16[512,2048]{1,0:T(8,128)(2,1)S(1)} %copy-done, bf16[2048,2048]{1,0:T(8,128)(2,1)} %param.11), kind=kOutput, calls=%fused_computation.68 | convolution fusion | flops 4297064448 | bytes 16777216 | tf_op jit(solution)/shard_map/dot_general | solution.py:163
  207.3 5.3 %copy.81 = f32[512,2048]{0,1:T(8,128)} copy(f32[512,2048]{1,0:T(8,128)} %convert_add_fusion) | data formatting | bytes 8388608 | tf_op jit(solution)/shard_map/add | solution.py:163
  212.6 2.9 %add_convert_fusion = (bf16[512,32,32]{0,2,1:T(8,128)(2,1)S(1)}, bf16[512,32,32]{0,2,1:T(8,128)(2,1)S(1)}) fusion(f32[512,32,64]{0,2,1:T(8,128)} %bitcast.785, f32[512,32]{0,1:T(8,128)S(1)} %get-tuple-element.17, f32[512,32]{0,1:T(8,128)S(1)} %get-tuple-element.16), kind=kLoop, calls=%fused_computation.121 | loop fusion | flops 4194304 | bytes 6422528 | tf_op jit(solution)/shard_map/convert.33
  253.7 2.1 copy.87
  261.5 2.1 copy.86
  268.4 2.9 %pad_maximum_fusion.1 = bf16[512,2048]{1,0:T(8,128)(2,1)} fusion(bf16[128,2048]{1,0:T(8,128)(2,1)} %copy.88, bf16[128,2048]{1,0:T(8,128)(2,1)} %copy.87, bf16[128,2048]{1,0:T(8,128)(2,1)} %copy.86, bf16[128,2048]{1,0:T(8,128)(2,1)S(1)} %copy.85), kind=kLoop, calls=%fused_computation.120 | loop fusion | flops 8388608 | bytes 4194304 | tf_op jit(solution)/shard_map/concatenate | solution.py:106
  (228 shorter events, 66.5 us)
Async XLA Ops:
  6.5 4.1 %copy-start = (bf16[512,2048]{1,0:T(8,128)(2,1)S(1)}, bf16[512,2048]{1,0:T(8,128)(2,1)}, u32[]{:S(2)}) copy-start(bf16[512,2048]{1,0:T(8,128)(2,1)} %param.10) | copy-start | bytes 6291460
  6.5 98.7 %all-gather.4.cloned.1.call-start = ((), (), s32[]{:S(2)}) async-start(), calls=%async_computation.3 | async-start | bytes 4718592 | tf_op jit(solution)/shard_map/all_gather | solution.py:148
  21.3 9.0 %copy-start.32 = (bf16[32,16,64]{2,1,0:T(8,128)(2,1)S(1)}, bf16[32,16,64]{2,1,0:T(8,128)(2,1)}, u32[]{:S(2)}) copy-start(bf16[32,16,64]{2,1,0:T(8,128)(2,1)} %param.16) | copy-start | bytes 196612
  21.3 88.1 %all-to-all-start = ((bf16[16,64,2048]{2,1,0:T(8,128)(2,1)}), bf16[16,64,2048]{2,1,0:T(8,128)(2,1)}, u32[]{:S(2)}, u32[]{:S(2)}) async-start(bf16[16,64,2048]{2,1,0:T(8,128)(2,1)} %broadcast_select_fusion), calls=%async_computation | async-start | bytes 8388608 | tf_op jit(solution)/shard_map/all_to_all | solution.py:155
  29.6 90.1 %all-gather.6.cloned.1.call-start = ((), (), s32[]{:S(2)}) async-start(), calls=%async_computation.4 | async-start | bytes 2359296 | tf_op jit(solution)/shard_map/all_gather | solution.py:149
  30.6 24.6 %copy-start.35 = (s32[1,16]{1,0:T(1,128)S(1)}, s32[1,16]{1,0:T(1,128)}, u32[]{:S(2)}) copy-start(s32[1,16]{1,0:T(1,128)} %param.18) | copy-start | bytes 196
  30.6 73.4 %copy-start.33 = (s32[512]{0:T(512)S(1)}, s32[512]{0:T(512)}, u32[]{:S(2)}) copy-start(s32[512]{0:T(512)} %param.17) | copy-start | bytes 6148
  115.0 18.8 %all-to-all-start.1 = ((bf16[16,64,512]{2,1,0:T(8,128)(2,1)}), bf16[16,64,512]{2,1,0:T(8,128)(2,1)}, u32[]{:S(2)}, u32[]{:S(2)}) async-start(bf16[16,64,512]{2,1,0:T(8,128)(2,1)} %convolution_convert_fusion.1), calls=%async_computation.1 | async-start | bytes 2097152 | tf_op jit(solution)/shard_map/all_to_all | solution.py:159
  133.8 55.8 %all-to-all-start.2 = ((bf16[16,64,2048]{2,1,0:T(8,128)(2,1)}), bf16[16,64,2048]{2,1,0:T(8,128)(2,1)}, u32[]{:S(2)}, u32[]{:S(2)}) async-start(bf16[16,64,2048]{2,1,0:T(8,128)(2,1)} %convolution_convert_fusion), calls=%async_computation.2 | async-start | bytes 8388608 | tf_op jit(solution)/shard_map/all_to_all | solution.py:158
  138.8 3.4 %copy-start.34 = (s32[512]{0:T(512)}, s32[512]{0:T(512)S(1)}, u32[]{:S(2)}) copy-start(s32[512]{0:T(512)S(1)} %iota.56) | copy-start | bytes 6148
  244.2 3.7 %copy-start.24 = (f32[4,128,192]{1,2,0:T(8,128)S(1)}, f32[4,128,192]{1,2,0:T(8,128)}, u32[]{:S(2)}) copy-start(f32[4,128,192]{1,2,0:T(8,128)} %get-tuple-element.43) | copy-start | bytes 1179652
  244.5 4.5 %copy-start.23 = (f32[4,128,192]{1,2,0:T(8,128)S(1)}, f32[4,128,192]{1,2,0:T(8,128)}, u32[]{:S(2)}) copy-start(f32[4,128,192]{1,2,0:T(8,128)} %get-tuple-element.45) | copy-start | bytes 1179652
  244.9 5.3 %copy-start.22 = (f32[4,128,192]{1,2,0:T(8,128)S(1)}, f32[4,128,192]{1,2,0:T(8,128)}, u32[]{:S(2)}) copy-start(f32[4,128,192]{1,2,0:T(8,128)} %get-tuple-element.47) | copy-start | bytes 1179652
  245.9 5.4 %copy-start.21 = (f32[4,128,192]{1,2,0:T(8,128)S(1)}, f32[4,128,192]{1,2,0:T(8,128)}, u32[]{:S(2)}) copy-start(f32[4,128,192]{1,2,0:T(8,128)} %get-tuple-element.49) | copy-start | bytes 1179652
  248.0 3.4 %copy-start.30 = (bf16[192,512]{0,1:T(8,128)(2,1)S(1)}, bf16[192,512]{0,1:T(8,128)(2,1)}, u32[]{:S(2)}) copy-start(bf16[192,512]{0,1:T(8,128)(2,1)} %copy.83) | copy-start | bytes 589828
  248.0 3.6 %copy-start.20 = (f32[4,128,192]{1,2,0:T(8,128)S(1)}, f32[4,128,192]{1,2,0:T(8,128)}, u32[]{:S(2)}) copy-start(f32[4,128,192]{1,2,0:T(8,128)} %get-tuple-element.51) | copy-start | bytes 1179652
  252.0 3.8 %copy-start.16 = (f32[4,128,192]{1,2,0:T(8,128)S(1)}, f32[4,128,192]{1,2,0:T(8,128)}, u32[]{:S(2)}) copy-start(f32[4,128,192]{1,2,0:T(8,128)} %get-tuple-element.59) | copy-start | bytes 1179652
  252.3 4.5 %copy-start.15 = (f32[4,128,192]{1,2,0:T(8,128)S(1)}, f32[4,128,192]{1,2,0:T(8,128)}, u32[]{:S(2)}) copy-start(f32[4,128,192]{1,2,0:T(8,128)} %get-tuple-element.61) | copy-start | bytes 1179652
  252.6 5.3 %copy-start.14 = (f32[4,128,192]{1,2,0:T(8,128)S(1)}, f32[4,128,192]{1,2,0:T(8,128)}, u32[]{:S(2)}) copy-start(f32[4,128,192]{1,2,0:T(8,128)} %get-tuple-element.63) | copy-start | bytes 1179652
  253.7 5.4 %copy-start.13 = (f32[4,128,192]{1,2,0:T(8,128)S(1)}, f32[4,128,192]{1,2,0:T(8,128)}, u32[]{:S(2)}) copy-start(f32[4,128,192]{1,2,0:T(8,128)} %get-tuple-element.65) | copy-start | bytes 1179652
  255.9 3.6 %copy-start.12 = (f32[4,128,192]{1,2,0:T(8,128)S(1)}, f32[4,128,192]{1,2,0:T(8,128)}, u32[]{:S(2)}) copy-start(f32[4,128,192]{1,2,0:T(8,128)} %get-tuple-element.67) | copy-start | bytes 1179652
  259.8 3.8 %copy-start.8 = (f32[4,128,192]{1,2,0:T(8,128)S(1)}, f32[4,128,192]{1,2,0:T(8,128)}, u32[]{:S(2)}) copy-start(f32[4,128,192]{1,2,0:T(8,128)} %get-tuple-element.75) | copy-start | bytes 1179652
  260.1 3.7 %copy-start.7 = (f32[4,128,192]{1,2,0:T(8,128)S(1)}, f32[4,128,192]{1,2,0:T(8,128)}, u32[]{:S(2)}) copy-start(f32[4,128,192]{1,2,0:T(8,128)} %get-tuple-element.77) | copy-start | bytes 1179652
  267.0 4.3 %copy-start.1 = (bf16[512,2048]{1,0:T(8,128)(2,1)S(1)}, bf16[512,2048]{1,0:T(8,128)(2,1)}, u32[]{:S(2)}) copy-start(bf16[512,2048]{1,0:T(8,128)(2,1)} %param.10) | copy-start | bytes 6291460
  (19 other events, 28.9 us)
Sparse Core Ops, SparseCore 0:
  9.0 44.3 all-gather.3
  55.1 27.0 all-gather.5
where the time goes:
time: 279 us; the launch traced here: 278 us
  blocking collectives  70.2 us (25%)
  matrix products  64.4 us (23%)
  local copies, waits for them, and re-layouts  55.3 us (20%)
  waiting for transfers between devices  38.3 us (14%)
  other arithmetic  17.9 us (6%)
  starting transfers between devices  17.6 us (6%)
  between operations  14.4 us (5%)
    all_gather x1, blocking collectives, local(): lax.all_gather(adapter_per_request, 'store', axis=0, tiled=True)  48.8 us
    all_to_all x1, waiting for transfers between devices, local(): lax.all_to_all(query_update, 'store', split_axis=0, concat_axis=0, tiled=...  30.4 us
    dot_general x32, matrix products, attention(): jnp.einsum('qhd,kd->hqk', query_part, key_part, preferred_element_type=jn...  26.6 us
    all_gather x1, blocking collectives, local(): lax.all_gather(adapter_up_value_weight, 'serve', axis=2, tiled=True)  21.4 us
    dot_general x32, matrix products, attention(): jnp.einsum('hqk,kd->qhd', weights, value_part, preferred_element_type=jnp...  11.5 us
    dot_general x1, matrix products, local(): jnp.dot(normalized_hidden_states, query_weight_matrix, preferred_element_...  9.7 us
    all_to_all x1, starting transfers between devices, local(): lax.all_to_all(block_list, 'store', split_axis=0, concat_axis=0, tiled=True)  8.28 us
    gather x1, local copies, waits for them, and re-layouts, local(): delta_query = query_update.reshape(-1, query_update.shape[2])[back_index]  7.95 us
  transfers between devices with their start and end apart: 5, of which 2 were waited for; matrix products, arithmetic and copies ran while one was open for 20% of the time, Pallas kernels for 0%

commit v1 on v0

--- a/solution.py
+++ b/solution.py
@@ -9,6 +9,26 @@
 ADAPTER_RANK = 16
 ADP_DEV = 32
 LEN_MAX = 64
+
+
+def process_pairs_all(view):
+    bus_axis = "serve"
+    kept_rows = []
+    world = lax.psum(1, bus_axis)
+    for h in range(world):
+        kept_rows.append((h, (h + 1) % world))
+    buffers = []
+    for h in range(world):
+        buffers.append((h, (h - 1) % world))
+    small, local_part = ([view], [view])
+    for _ in range(world // 2):
+        small.append(lax.ppermute(small[-1], bus_axis, kept_rows))
+    for _ in range((world - 1) // 2):
+        y_new = lax.ppermute(local_part[-1], bus_axis, buffers)
+        local_part.append(y_new)
+    before = jnp.concatenate([*small[::-1], *local_part[1:]], axis=2)
+    next_value = lax.axis_index(bus_axis)
+    return jnp.roll(before, (next_value - world // 2) * view.shape[2], axis=2)
 
 
 def rotary(heads_in, positions):
@@ -147,7 +167,7 @@
     panels = (
         lax.all_gather(adapter_down_weight, "serve", axis=2, tiled=True),
         lax.all_gather(adapter_up_query_weight, "serve", axis=2, tiled=True),
-        lax.all_gather(adapter_up_value_weight, "serve", axis=2, tiled=True),
+        process_pairs_all(adapter_up_value_weight),
     )
     down_chosen, upq_chosen, upv_chosen = local_choice(
         panels, group_lists, adapter_panel_slot, my_store

time: 279 us -> 313 us (1.12)
  waiting for transfers between devices: 38.3 us -> 61 us
  starting transfers between devices: 17.6 us -> 22.8 us
  local copies, waits for them, and re-layouts: 55.3 us -> 59 us
    all_gather x1, blocking collectives: 48.8 us -> 71.9 us  [local(): lax.all_gather(adapter_per_request, 'store', axis=0, tiled=True)]
    all_gather x1 -> x0, blocking collectives: 21.4 us -> none  [local(): lax.all_gather(adapter_up_value_weight, 'serve', axis=2, tiled=True)]
    all_to_all x1, waiting for transfers between devices: 30.4 us -> 40.2 us  [local(): lax.all_to_all(query_update, 'store', split_axis=0, concat_axis=0, tiled=...]
    ppermute x0 -> x7, waiting for transfers between devices: none -> 8.45 us  [the longest x4 8.45 us: process_pairs_all(): small.append(lax.ppermute(small[-1], bus_axis, kept_rows))]
    ppermute x0 -> x7, starting transfers between devices: none -> 5.21 us  [the longest x3 5.17 us: process_pairs_all(): y_new = lax.ppermute(local_part[-1], bus_axis, buffers)]
    all_to_all x1, waiting for transfers between devices: 6.49 us -> 10.8 us  [local(): lax.all_to_all(value_update, 'store', split_axis=0, concat_axis=0, tiled=...]
  transfers between devices with their start and end apart: 5 -> 12, of which waited for: 2 -> 5; matrix products, arithmetic and copies ran while one was open for 20% -> 19% of each run, Pallas kernels for 0% -> 0%
where the time goes in v1:
time: 313 us; the launch traced here: 311 us
  blocking collectives  71.9 us (23%)
  matrix products  64.3 us (21%)
  waiting for transfers between devices  61 us (19%)
  local copies, waits for them, and re-layouts  59 us (19%)
  starting transfers between devices  22.8 us (7%)
  other arithmetic  17.9 us (6%)
  between operations  14.4 us (5%)
    all_gather x1, blocking collectives, local(): lax.all_gather(adapter_per_request, 'store', axis=0, tiled=True)  71.9 us
    all_to_all x1, waiting for transfers between devices, local(): lax.all_to_all(query_update, 'store', split_axis=0, concat_axis=0, tiled=...  40.2 us
    dot_general x32, matrix products, attention(): jnp.einsum('qhd,kd->hqk', query_part, key_part, preferred_element_type=jn...  26.6 us
    dot_general x32, matrix products, attention(): jnp.einsum('hqk,kd->qhd', weights, value_part, preferred_element_type=jnp...  11.5 us
    all_to_all x1, waiting for transfers between devices, local(): lax.all_to_all(value_update, 'store', split_axis=0, concat_axis=0, tiled=...  10.8 us
    dot_general x1, matrix products, local(): jnp.dot(normalized_hidden_states, query_weight_matrix, preferred_element_...  9.7 us
    gather x3, local copies, waits for them, and re-layouts, local_choice(): return tuple((jnp.take(panel, local_source, axis=0) for panel in panel_set))  8.96 us
    ppermute x4, waiting for transfers between devices, process_pairs_all(): small.append(lax.ppermute(small[-1], bus_axis, kept_rows))  8.45 us
  transfers between devices with their start and end apart: 12, of which 5 were waited for; matrix products, arithmetic and copies ran while one was open for 19% of the time, Pallas kernels for 0%

profile of v1, /device:TPU:6, one launch (start us, length us, event | category | flops | bytes accessed | tf_op | source)
XLA Modules:
  0.0 311.3 jit_solution(16584328445695789760)
XLA Ops:
  10.6 6.1 %gather_fusion = bf16[1024,2048]{1,0:T(8,128)(2,1)} fusion(bf16[512,2048]{1,0:T(8,128)(2,1)S(1)} %copy-done, s32[1024]{0:T(1024)S(1)} %broadcast_clamp_fusion), kind=kCustom, calls=%fused_computation | custom fusion | bytes 8392704 | tf_op jit(solution)/shard_map/gather | solution.py:163
  16.8 4.5 %broadcast_select_fusion = bf16[16,64,2048]{2,1,0:T(8,128)(2,1)} fusion(bf16[16,64,2048]{2,1,0:T(8,128)(2,1)} %bitcast.785, pred[16,64]{1,0:T(8,128)(4,1)S(1)} %iota_compare_fusion.6), kind=kLoop, calls=%fused_computation.69 | loop fusion | flops 2097152 | bytes 8389632 | tf_op jit(solution)/shard_map/jit(_where)/select_n | solution.py:162
  21.3 8.3 %all-to-all-start = ((bf16[16,64,2048]{2,1,0:T(8,128)(2,1)}), bf16[16,64,2048]{2,1,0:T(8,128)(2,1)}, u32[]{:S(2)}, u32[]{:S(2)}) async-start(bf16[16,64,2048]{2,1,0:T(8,128)(2,1)} %broadcast_select_fusion), calls=%async_computation | async-start | bytes 8388608 | tf_op jit(solution)/shard_map/all_to_all | solution.py:175
  32.1 71.9 %all-gather = s32[16,1,16]{2,1,0:T(1,128)S(1)} all-gather(s32[1,1,16]{2,1,0:T(1,128)S(1)} %bitcast.855), channel_id=1, replica_groups=mesh['serve'=8,'store'=16] {'store'}, dimensions={0}, use_global_device_ids=true | all-gather | bytes 1088 | tf_op jit(solution)/shard_map/all_gather | solution.py:145
  106.4 2.6 collective-permute-done.1
  110.8 2.6 collective-permute-done.2
  114.7 3.2 %collective-permute-done.3 = bf16[32,16,64]{2,1,0:T(8,128)(2,1)} collective-permute-done((bf16[32,16,64]{2,1,0:T(8,128)(2,1)S(1)}, bf16[32,16,64]{2,1,0:T(8,128)(2,1)}, u32[]{:S(2)}, u32[]{:S(2)}) %collective-permute-start.3) | collective-permute-done | bytes 65568 | tf_op jit(solution)/shard_map/ppermute | solution.py:25
  117.9 2.6 concatenate.43
  123.3 4.2 %gather_fusion.1 = bf16[16,32,2048]{2,1,0:T(8,128)(2,1)} fusion(bf16[32,32,2048]{2,1,0:T(8,128)(2,1)} %all-gather.4.cloned.1.call-done, s32[1024]{0:T(1024)S(1)} %pad_clamp_fusion.1), kind=kCustom, calls=%fused_computation.1 | custom fusion | bytes 4194368 | tf_op jit(solution)/shard_map/jit(_take)/gather | solution.py:73
  127.5 4.1 %fusion.68 = bf16[16,64,32]{1,2,0:T(8,128)(2,1)S(1)} fusion(bf16[16,64,2048]{2,1,0:T(8,128)(2,1)} %all-to-all-done, bf16[16,32,2048]{2,1,0:T(8,128)(2,1)} %gather_fusion.1, pred[16]{0:T(512)(128)(4,1)S(1)} %compare_and_fusion.4), kind=kOutput, calls=%fused_computation.225 | convolution fusion | flops 135299072 | bytes 6357008 | tf_op jit(solution)/shard_map/jkd,jrd->jkr/dot_general | solution.py:57
  133.1 4.5 %all-to-all-start.1 = ((bf16[16,64,512]{2,1,0:T(8,128)(2,1)}), bf16[16,64,512]{2,1,0:T(8,128)(2,1)S(1)}, u32[]{:S(2)}, u32[]{:S(2)}) async-start(bf16[16,64,512]{2,1,0:T(8,128)(2,1)} %convolution_convert_fusion.1), calls=%async_computation.1 | async-start | bytes 2097152 | tf_op jit(solution)/shard_map/all_to_all | solution.py:179
  137.7 3.2 %gather_fusion.4 = bf16[16,16,2048]{2,1,0:T(8,128)(2,1)} fusion(bf16[32,16,2048]{2,1,0:T(8,128)(2,1)} %all-gather.6.cloned.1.call-done, s32[1024]{0:T(1024)S(1)} %pad_clamp_fusion.1), kind=kCustom, calls=%fused_computation.4 | custom fusion | bytes 2097216 | tf_op jit(solution)/shard_map/jit(_take)/gather | solution.py:73
  140.9 4.5 %convolution_convert_fusion = bf16[16,64,2048]{2,1,0:T(8,128)(2,1)} fusion(bf16[16,16,2048]{2,1,0:T(8,128)(2,1)} %gather_fusion.4, pred[16]{0:T(512)(128)(4,1)S(1)} %compare_and_fusion.4, bf16[16,64,32]{1,2,0:T(8,128)(2,1)S(1)} %fusion.68), kind=kOutput, calls=%fused_computation.70 | convolution fusion | flops 69730304 | bytes 5308928 | tf_op jit(solution)/shard_map/jkr,jrd->jkd/dot_general | solution.py:60
  145.3 10.8 %all-to-all-done.1 = bf16[16,64,512]{2,1,0:T(8,128)(2,1)S(1)} async-done(((bf16[16,64,512]{2,1,0:T(8,128)(2,1)}), bf16[16,64,512]{2,1,0:T(8,128)(2,1)S(1)}, u32[]{:S(2)}, u32[]{:S(2)}) %all-to-all-start.1) | async-done | bytes 1048608 | tf_op jit(solution)/shard_map/all_to_all | solution.py:179
  157.1 4.7 %all-to-all-start.2 = ((bf16[16,64,2048]{2,1,0:T(8,128)(2,1)}), bf16[16,64,2048]{2,1,0:T(8,128)(2,1)}, u32[]{:S(2)}, u32[]{:S(2)}) async-start(bf16[16,64,2048]{2,1,0:T(8,128)(2,1)} %convolution_convert_fusion), calls=%async_computation.2 | async-start | bytes 8388608 | tf_op jit(solution)/shard_map/all_to_all | solution.py:178
  162.6 2.9 fusion.563
  167.1 3.3 %gather_fusion.3 = bf16[512,512]{1,0:T(8,128)(2,1)S(1)} fusion(bf16[1024,512]{1,0:T(8,128)(2,1)} %bitcast.784, s32[1024]{0:T(1024)S(1)} %pad_clamp_fusion), kind=kCustom, calls=%fused_computation.3 | custom fusion | bytes 1050624 | tf_op jit(solution)/shard_map/gather | solution.py:182
  170.4 3.6 %fusion.3 = bf16[512,512]{1,0:T(8,128)(2,1)} fusion(bf16[512,2048]{1,0:T(8,128)(2,1)S(1)} %copy-done, bf16[2048,512]{1,0:T(8,128)(2,1)} %param.13, bf16[512,512]{1,0:T(8,128)(2,1)S(1)} %gather_fusion.3), kind=kOutput, calls=%fused_computation.128 | convolution fusion | flops 1074528256 | bytes 5242880 | tf_op jit(solution)/shard_map/dot_general | solution.py:194
  182.6 40.2 %all-to-all-done.2 = bf16[16,64,2048]{2,1,0:T(8,128)(2,1)} async-done(((bf16[16,64,2048]{2,1,0:T(8,128)(2,1)}), bf16[16,64,2048]{2,1,0:T(8,128)(2,1)}, u32[]{:S(2)}, u32[]{:S(2)}) %all-to-all-start.2) | async-done | bytes 4194336 | tf_op jit(solution)/shard_map/all_to_all | solution.py:178
  222.9 8.0 %gather_fusion.5 = bf16[512,2048]{1,0:T(8,128)(2,1)} fusion(bf16[1024,2048]{1,0:T(8,128)(2,1)} %bitcast.19, s32[1024]{0:T(1024)S(1)} %pad_clamp_fusion), kind=kCustom, calls=%fused_computation.5 | custom fusion | bytes 4196352 | tf_op jit(solution)/shard_map/gather | solution.py:181
  230.8 9.7 %convert_add_fusion = f32[512,2048]{1,0:T(8,128)} fusion(bf16[512,2048]{1,0:T(8,128)(2,1)} %gather_fusion.5, bf16[512,2048]{1,0:T(8,128)(2,1)S(1)} %copy-done, bf16[2048,2048]{1,0:T(8,128)(2,1)} %param.11), kind=kOutput, calls=%fused_computation.68 | convolution fusion | flops 4297064448 | bytes 16777216 | tf_op jit(solution)/shard_map/dot_general | solution.py:183
  240.5 5.3 %copy.65 = f32[512,2048]{0,1:T(8,128)} copy(f32[512,2048]{1,0:T(8,128)} %convert_add_fusion) | data formatting | bytes 8388608 | tf_op jit(solution)/shard_map/add | solution.py:183
  245.9 2.9 add_convert_fusion
  301.6 2.9 pad_maximum_fusion.1
  (255 shorter events, 80.1 us)
Async XLA Ops:
  6.5 116.7 %all-gather.4.cloned.1.call-start = ((), (), s32[]{:S(2)}) async-start(), calls=%async_computation.3 | async-start | bytes 4718592 | tf_op jit(solution)/shard_map/all_gather | solution.py:168
  21.3 9.0 %copy-start.27 = (bf16[32,16,64]{2,1,0:T(8,128)(2,1)S(1)}, bf16[32,16,64]{2,1,0:T(8,128)(2,1)}, u32[]{:S(2)}) copy-start(bf16[32,16,64]{2,1,0:T(8,128)(2,1)} %param.16) | copy-start | bytes 196612
  21.3 10.8 %copy-start.42 = (s32[1,16]{1,0:T(1,128)S(1)}, s32[1,16]{1,0:T(1,128)}, u32[]{:S(2)}) copy-start(s32[1,16]{1,0:T(1,128)} %param.18) | copy-start | bytes 196
  21.3 82.7 %copy-start.38 = (s32[512]{0:T(512)S(1)}, s32[512]{0:T(512)}, u32[]{:S(2)}) copy-start(s32[512]{0:T(512)} %param.17) | copy-start | bytes 6148
  21.3 106.2 %all-to-all-start = ((bf16[16,64,2048]{2,1,0:T(8,128)(2,1)}), bf16[16,64,2048]{2,1,0:T(8,128)(2,1)}, u32[]{:S(2)}, u32[]{:S(2)}) async-start(bf16[16,64,2048]{2,1,0:T(8,128)(2,1)} %broadcast_select_fusion), calls=%async_computation | async-start | bytes 8388608 | tf_op jit(solution)/shard_map/all_to_all | solution.py:175
  29.6 108.1 %all-gather.6.cloned.1.call-start = ((), (), s32[]{:S(2)}) async-start(), calls=%async_computation.4 | async-start | bytes 2359296 | tf_op jit(solution)/shard_map/all_gather | solution.py:169
  30.3 74.3 %collective-permute-start = (bf16[32,16,64]{2,1,0:T(8,128)(2,1)S(1)}, bf16[32,16,64]{2,1,0:T(8,128)(2,1)S(1)}, u32[]{:S(2)}, u32[]{:S(2)}) collective-permute-start(bf16[32,16,64]{2,1,0:T(8,128)(2,1)S(1)} %copy-done.27), channel_id=1, source_target_pairs={{0,16},{16,32},{32,48},{48,64},{64,80},{80,96},{96,112},{112,0},{1... | collective-permute-start | bytes 196616 | tf_op jit(solution)/shard_map/ppermute | solution.py:25
  30.4 74.3 %collective-permute-start.4 = (bf16[32,16,64]{2,1,0:T(8,128)(2,1)S(1)}, bf16[32,16,64]{2,1,0:T(8,128)(2,1)S(1)}, u32[]{:S(2)}, u32[]{:S(2)}) collective-permute-start(bf16[32,16,64]{2,1,0:T(8,128)(2,1)S(1)} %copy-done.27), channel_id=1, source_target_pairs={{0,112},{16,0},{32,16},{48,32},{64,48},{80,64},{96,80},{112,96},{1... | collective-permute-start | bytes 196616 | tf_op jit(solution)/shard_map/ppermute | solution.py:27
  104.6 4.4 %collective-permute-start.1 = (bf16[32,16,64]{2,1,0:T(8,128)(2,1)S(1)}, bf16[32,16,64]{2,1,0:T(8,128)(2,1)S(1)}, u32[]{:S(2)}, u32[]{:S(2)}) collective-permute-start(bf16[32,16,64]{2,1,0:T(8,128)(2,1)S(1)} %collective-permute-done), channel_id=1, source_target_pairs={{0,16},{16,32},{32,48},{48,64},{64,80},{80,96},{96,112},{112,0},{1... | collective-permute-start | bytes 196616 | tf_op jit(solution)/shard_map/ppermute | solution.py:25
  104.6 4.4 %collective-permute-start.5 = (bf16[32,16,64]{2,1,0:T(8,128)(2,1)S(1)}, bf16[32,16,64]{2,1,0:T(8,128)(2,1)S(1)}, u32[]{:S(2)}, u32[]{:S(2)}) collective-permute-start(bf16[32,16,64]{2,1,0:T(8,128)(2,1)S(1)} %collective-permute-done.4), channel_id=1, source_target_pairs={{0,112},{16,0},{32,16},{48,32},{64,48},{80,64},{96,80},{112,96},{1... | collective-permute-start | bytes 196616 | tf_op jit(solution)/shard_map/ppermute | solution.py:27
  109.0 4.4 %copy-start.28 = (bf16[32,16,64]{2,1,0:T(8,128)(2,1)}, bf16[32,16,64]{2,1,0:T(8,128)(2,1)S(1)}, u32[]{:S(2)}) copy-start(bf16[32,16,64]{2,1,0:T(8,128)(2,1)S(1)} %collective-permute-done.1) | copy-start | bytes 196612
  109.0 4.4 %collective-permute-start.2 = (bf16[32,16,64]{2,1,0:T(8,128)(2,1)S(1)}, bf16[32,16,64]{2,1,0:T(8,128)(2,1)S(1)}, u32[]{:S(2)}, u32[]{:S(2)}) collective-permute-start(bf16[32,16,64]{2,1,0:T(8,128)(2,1)S(1)} %collective-permute-done.1), channel_id=1, source_target_pairs={{0,16},{16,32},{32,48},{48,64},{64,80},{80,96},{96,112},{112,0},{1... | collective-permute-start | bytes 196616 | tf_op jit(solution)/shard_map/ppermute | solution.py:25
  109.0 4.4 %copy-start.29 = (bf16[32,16,64]{2,1,0:T(8,128)(2,1)}, bf16[32,16,64]{2,1,0:T(8,128)(2,1)S(1)}, u32[]{:S(2)}) copy-start(bf16[32,16,64]{2,1,0:T(8,128)(2,1)S(1)} %collective-permute-done.5) | copy-start | bytes 196612
  109.1 4.4 %collective-permute-start.6 = (bf16[32,16,64]{2,1,0:T(8,128)(2,1)S(1)}, bf16[32,16,64]{2,1,0:T(8,128)(2,1)S(1)}, u32[]{:S(2)}, u32[]{:S(2)}) collective-permute-start(bf16[32,16,64]{2,1,0:T(8,128)(2,1)S(1)} %collective-permute-done.5), channel_id=1, source_target_pairs={{0,112},{16,0},{32,16},{48,32},{64,48},{80,64},{96,80},{112,96},{1... | collective-permute-start | bytes 196616 | tf_op jit(solution)/shard_map/ppermute | solution.py:27
  113.4 4.5 %collective-permute-start.3 = (bf16[32,16,64]{2,1,0:T(8,128)(2,1)S(1)}, bf16[32,16,64]{2,1,0:T(8,128)(2,1)}, u32[]{:S(2)}, u32[]{:S(2)}) collective-permute-start(bf16[32,16,64]{2,1,0:T(8,128)(2,1)S(1)} %collective-permute-done.2), channel_id=1, source_target_pairs={{0,16},{16,32},{32,48},{48,64},{64,80},{80,96},{96,112},{112,0},{1... | collective-permute-start | bytes 196616 | tf_op jit(solution)/shard_map/ppermute | solution.py:25
  133.1 23.0 %all-to-all-start.1 = ((bf16[16,64,512]{2,1,0:T(8,128)(2,1)}), bf16[16,64,512]{2,1,0:T(8,128)(2,1)S(1)}, u32[]{:S(2)}, u32[]{:S(2)}) async-start(bf16[16,64,512]{2,1,0:T(8,128)(2,1)} %convolution_convert_fusion.1), calls=%async_computation.1 | async-start | bytes 2097152 | tf_op jit(solution)/shard_map/all_to_all | solution.py:179
  145.3 16.8 %copy-start.40 = (s32[16]{0:T(128)S(1)}, s32[16]{0:T(128)}, u32[]{:S(2)}) copy-start(s32[16]{0:T(128)} %copy-done.39) | copy-start | bytes 196
  157.1 65.8 %all-to-all-start.2 = ((bf16[16,64,2048]{2,1,0:T(8,128)(2,1)}), bf16[16,64,2048]{2,1,0:T(8,128)(2,1)}, u32[]{:S(2)}, u32[]{:S(2)}) async-start(bf16[16,64,2048]{2,1,0:T(8,128)(2,1)} %convolution_convert_fusion), calls=%async_computation.2 | async-start | bytes 8388608 | tf_op jit(solution)/shard_map/all_to_all | solution.py:178
  277.8 4.5 %copy-start.24 = (f32[4,128,192]{1,2,0:T(8,128)S(1)}, f32[4,128,192]{1,2,0:T(8,128)}, u32[]{:S(2)}) copy-start(f32[4,128,192]{1,2,0:T(8,128)} %get-tuple-element.45) | copy-start | bytes 1179652
  278.1 5.3 %copy-start.23 = (f32[4,128,192]{1,2,0:T(8,128)S(1)}, f32[4,128,192]{1,2,0:T(8,128)}, u32[]{:S(2)}) copy-start(f32[4,128,192]{1,2,0:T(8,128)} %get-tuple-element.47) | copy-start | bytes 1179652
  279.1 5.4 %copy-start.22 = (f32[4,128,192]{1,2,0:T(8,128)S(1)}, f32[4,128,192]{1,2,0:T(8,128)}, u32[]{:S(2)}) copy-start(f32[4,128,192]{1,2,0:T(8,128)} %get-tuple-element.49) | copy-start | bytes 1179652
  285.6 4.5 %copy-start.16 = (f32[4,128,192]{1,2,0:T(8,128)S(1)}, f32[4,128,192]{1,2,0:T(8,128)}, u32[]{:S(2)}) copy-start(f32[4,128,192]{1,2,0:T(8,128)} %get-tuple-element.61) | copy-start | bytes 1179652
  285.9 5.3 %copy-start.15 = (f32[4,128,192]{1,2,0:T(8,128)S(1)}, f32[4,128,192]{1,2,0:T(8,128)}, u32[]{:S(2)}) copy-start(f32[4,128,192]{1,2,0:T(8,128)} %get-tuple-element.63) | copy-start | bytes 1179652
  286.9 5.4 %copy-start.14 = (f32[4,128,192]{1,2,0:T(8,128)S(1)}, f32[4,128,192]{1,2,0:T(8,128)}, u32[]{:S(2)}) copy-start(f32[4,128,192]{1,2,0:T(8,128)} %get-tuple-element.65) | copy-start | bytes 1179652
  (33 other events, 71.0 us)
Sparse Core Ops, SparseCore 0:
  9.0 38.3 all-gather.3
  49.1 27.6 all-gather.5
